TPU v7x, 512 devices: a whole 4x8x8 slice. The times are simulated.
512 devices in a mesh: wide: 32 (over z, x), narrow: 16 (over y, core).
Axes of the slice: x: 4, y: 8, z: 8, core: 2. Of those that a mesh axis runs over, the one named last changes fastest.
Arguments:
- tokens: bfloat16 [1024, 16384], P('wide', 'narrow'), may hold values from -200 to 200
- norm_gain: float32 [16384], P('narrow'), may hold values from 0.25 to 1.75
- gate_weight: bfloat16 [26624, 16384], P('wide', 'narrow'), may hold values from -0.046875 to 0.046875
- up_weight: bfloat16 [26624, 16384], P('wide', 'narrow'), may hold values from -0.046875 to 0.046875
- down_weight: bfloat16 [26624, 16384], P('wide', 'narrow'), may hold values from -0.0390625 to 0.0390625
Outputs:
- ffn_out: bfloat16 [1024, 16384], P('wide', 'narrow')
All inputs are finite; a program needn't handle non-finite values.
Results may differ from a plain program's by a relative error of at most 0.03.
Values may be sent and summed in bfloat16 or wider, within the bound.
No kernel may reach another device: no remote copies, remote signals or barrier semaphores. Data moves between devices by JAX's collectives and lax.ppermute only.
A program may use at most 64 MiB of HBM per device.

v0:
```python
import jax
import jax.numpy as jnp
from jax import lax
from jax.sharding import PartitionSpec as P

D = 16384
EPS = 1e-05


def project_pair(rows, gate_weight, up_weight):
    dims = (((1,), (1,)), ((), ()))
    gate = lax.dot_general(rows, gate_weight, dims, preferred_element_type=jnp.float32)
    upward = lax.dot_general(rows, up_weight, dims, preferred_element_type=jnp.float32)
    return jnp.concatenate([gate, upward], axis=1)


def activate(sums, width):
    return (jax.nn.silu(sums[:, :width]) * sums[:, width:]).astype(jnp.bfloat16)


def local(tokens, norm_gain, gate_weight, up_weight, down_weight):
    width = gate_weight.shape[0]
    whole = lax.all_gather(tokens, "wide", axis=0, tiled=True)
    values = whole.astype(jnp.float32)
    squares = lax.psum(jnp.sum(values * values, axis=1), "narrow")
    normed = (values * lax.rsqrt(squares[:, None] / D + EPS) * norm_gain).astype(jnp.bfloat16)
    sums = lax.psum(
        project_pair(normed, gate_weight, up_weight).astype(jnp.bfloat16), "narrow"
    ).astype(jnp.float32)
    hidden = activate(sums, width)
    return lax.psum_scatter(
        jnp.dot(hidden, down_weight, preferred_element_type=jnp.float32).astype(jnp.bfloat16),
        "wide",
        scatter_dimension=0,
        tiled=True,
    )


def solution(mesh):
    in_specs = (
        P("wide", "narrow"),
        P("narrow"),
        P("wide", "narrow"),
        P("wide", "narrow"),
        P("wide", "narrow"),
    )
    out_specs = P("wide", "narrow")
    return jax.shard_map(local, mesh=mesh, in_specs=in_specs, out_specs=out_specs, check_vma=False)
```

profile of v0, /device:TPU:8, one launch (start us, length us, event | category | flops | bytes accessed | tf_op | source)
XLA Modules:
  0.0 490.7 jit_solution(1981325503855157326)
XLA Ops:
  6.5 0.0 copy-start
  6.5 0.0 all-gather.2.cloned.1.call-start
  6.5 0.7 all-gather.2.cloned.1.call-update
  7.3 0.0 all-reduce.2.cloned.1.call-start
  7.3 91.8 %all-gather.2.cloned.1.call-done = bf16[1024,1024]{1,0:T(8,128)(2,1)} async-done(((bf16[32,1024]{1,0:T(8,128)(2,1)}), bf16[1024,1024]{1,0:T(8,128)(2,1)}) %all-gather.2.cloned.1.call-update) | async-done | bytes 2097168 | tf_op jit(solution)/shard_map/all_gather | solution.py:23
  99.1 2.1 fusion
  101.2 20.6 %psum.14 = f32[1024]{0:T(1024)S(1)} all-reduce(f32[1024]{0:T(1024)S(1)} %fusion), channel_id=1, replica_groups=mesh['wide'=32,'narrow'=16] {'narrow'}, use_global_device_ids=true, to_apply=%region_1.0 | all-reduce | flops 1024 | bytes 8192 | tf_op jit(solution)/shard_map/psum | solution.py:25
  121.8 0.0 copy-start.1
  121.8 0.0 copy-start.2
  121.8 0.0 copy-start.3
  121.9 4.3 convolution_convert_fusion.1
  126.2 0.0 copy-done.1
  126.2 0.0 copy-done.2
  126.2 0.0 copy-done.3
  126.2 2.1 convolution_convert_fusion.2
  128.3 2.1 pad_maximum_fusion
  130.4 0.0 all-reduce.2.cloned.1.call-update
  130.4 0.0 reduce-scatter.2.cloned.1.call-start
  130.5 121.9 %all-reduce.2.cloned.1.call-done = bf16[1024,1664]{0,1:T(8,128)(2,1)} async-done(((bf16[1024,1664]{0,1:T(8,128)(2,1)}), bf16[1024,1664]{0,1:T(8,128)(2,1)}) %all-reduce.2.cloned.1.call-update) | async-done | bytes 3407888 | tf_op jit(solution)/shard_map/psum | solution.py:27
  252.4 2.8 convert_element_type.18
  255.2 0.0 copy-done
  255.2 3.9 convolution_convert_fusion
  259.0 0.0 reduce-scatter.2.cloned.1.call-update
  259.1 225.1 %reduce-scatter.2.cloned.1.call-done = bf16[32,1024]{1,0:T(8,128)(2,1)} async-done(((bf16[1024,1024]{1,0:T(8,128)(2,1)}), bf16[32,1024]{1,0:T(8,128)(2,1)}) %reduce-scatter.2.cloned.1.call-update) | async-done | bytes 65552 | tf_op jit(solution)/shard_map/reduce_scatter | solution.py:31
  (1 shorter events, 0.0 us)
Async XLA Ops:
  6.5 248.6 %copy-start = (bf16[832,1024]{1,0:T(8,128)(2,1)S(1)}, bf16[832,1024]{1,0:T(8,128)(2,1)}, u32[]{:S(2)}) copy-start(bf16[832,1024]{1,0:T(8,128)(2,1)} %param.9) | copy-start | bytes 5111812
  6.5 92.6 %all-gather.2.cloned.1.call-start = ((), (), s32[]{:S(2)}) async-start(), calls=%async_computation.1 | async-start | bytes 2162688 | tf_op jit(solution)/shard_map/all_gather | solution.py:23
  7.3 245.1 %all-reduce.2.cloned.1.call-start = ((), (), s32[]{:S(2)}) async-start(), calls=%async_computation.2 | async-start | bytes 6815744 | tf_op jit(solution)/shard_map/psum | solution.py:27
  121.8 4.3 copy-start.1
  121.8 4.3 copy-start.2
  121.8 4.3 copy-start.3
  130.4 353.8 %reduce-scatter.2.cloned.1.call-start = ((), (), s32[]{:S(2)}) async-start(), calls=%async_computation.3 | async-start | bytes 2162688 | tf_op jit(solution)/shard_map/reduce_scatter | solution.py:31
Sparse Core Ops, SparseCore 0:
  10.5 88.5 all-gather.1
  130.6 121.7 all-reduce.1
  259.2 224.9 reduce-scatter.1
where the time goes:
time: 491 us
  waiting for transfers between devices  440 us (90%)
  blocking collectives  20.6 us (4%)
  between operations  13.2 us (3%)
  matrix products  10.3 us (2%)
  other arithmetic  6.94 us (1%)
    reduce_scatter x1, waiting for transfers between devices, local(): lax.psum_scatter(jnp.dot(hidden, down_weight, preferred_element_type=jnp....  225 us
    psum x1, waiting for transfers between devices, local(): lax.psum(project_pair(normed, gate_weight, up_weight).astype(jnp.bfloat16...  122 us
    all_gather x1, waiting for transfers between devices, local(): whole = lax.all_gather(tokens, 'wide', axis=0, tiled=True)  91.8 us
    psum x1, blocking collectives, local(): squares = lax.psum(jnp.sum(values * values, axis=1), 'narrow')  20.6 us
  transfers between devices with their start and end apart: 3, of which 3 were waited for; matrix products, arithmetic and copies ran while one was open for 0% of the time, Pallas kernels for 0%

commit v1 on v0

--- a/solution.py
+++ b/solution.py
@@ -20,7 +20,10 @@
 
 def local(tokens, norm_gain, gate_weight, up_weight, down_weight):
     width = gate_weight.shape[0]
-    whole = lax.all_gather(tokens, "wide", axis=0, tiled=True)
+    size = lax.axis_size("wide")
+    shards = jnp.stack([tokens for _ in range(size)])
+    shards = lax.all_to_all(shards, "wide", split_axis=0, concat_axis=0)
+    whole = jnp.concatenate(shards, axis=0)
     values = whole.astype(jnp.float32)
     squares = lax.psum(jnp.sum(values * values, axis=1), "narrow")
     normed = (values * lax.rsqrt(squares[:, None] / D + EPS) * norm_gain).astype(jnp.bfloat16)

time: 491 us -> 463 us (0.943)
  waiting for transfers between devices: 440 us -> 346 us
  blocking collectives: 20.6 us -> 84.8 us
    all_gather x1 -> x0, waiting for transfers between devices: 91.8 us -> none  [local(): whole = lax.all_gather(tokens, 'wide', axis=0, tiled=True)]
    all_to_all x0 -> x1, blocking collectives: none -> 63.5 us  [local(): shards = lax.all_to_all(shards, 'wide', split_axis=0, concat_axis=0)]
  transfers between devices with their start and end apart: 3 -> 2, of which waited for: 3 -> 2; matrix products, arithmetic and copies ran while one was open for 0% -> 0% of each run, Pallas kernels for 0% -> 0%
where the time goes in v1:
time: 463 us
  waiting for transfers between devices  346 us (75%)
  blocking collectives  84.8 us (18%)
  between operations  13.5 us (3%)
  matrix products  7.9 us (2%)
  other arithmetic  7.6 us (2%)
    reduce_scatter x1, waiting for transfers between devices, local(): lax.psum_scatter(jnp.dot(hidden, down_weight, preferred_element_type=jnp....  225 us
    psum x1, waiting for transfers between devices, local(): lax.psum(project_pair(normed, gate_weight, up_weight).astype(jnp.bfloat16...  121 us
    all_to_all x1, blocking collectives, local(): shards = lax.all_to_all(shards, 'wide', split_axis=0, concat_axis=0)  63.5 us
    psum x1, blocking collectives, local(): squares = lax.psum(jnp.sum(values * values, axis=1), 'narrow')  21.2 us
  transfers between devices with their start and end apart: 2, of which 2 were waited for; matrix products, arithmetic and copies ran while one was open for 0% of the time, Pallas kernels for 0%

profile of v1, /device:TPU:8, one launch (start us, length us, event | category | flops | bytes accessed | tf_op | source)
XLA Modules:
  0.0 462.8 jit_solution(7485414060389519266)
XLA Ops:
  6.5 0.0 copy-start
  6.5 0.0 all-reduce.2.cloned.1.call-start
  6.5 1.2 stack.2
  7.8 63.5 %all_to_all.5 = bf16[32,32,1024]{2,1,0:T(8,128)(2,1)S(1)} all-to-all(bf16[32,32,1024]{2,1,0:T(8,128)(2,1)S(1)} %stack.2), channel_id=1, replica_groups=mesh['wide'=32,'narrow'=16] {'wide'}, dimensions={0} | all-to-all | bytes 4194304 | tf_op jit(solution)/shard_map/all_to_all | solution.py:25
  71.3 0.0 copy-start.1
  71.3 1.3 copy-done.1
  72.6 0.0 copy-start.2
  72.6 0.5 multiply_reduce_fusion
  73.1 0.1 reduce_sum.12
  73.2 21.2 %psum.14 = f32[1024]{0:T(1024)S(1)} all-reduce(f32[1024]{0:T(1024)S(1)} %reduce_sum.12), channel_id=1, replica_groups=mesh['wide'=32,'narrow'=16] {'narrow'}, use_global_device_ids=true, to_apply=%region_1.0 | all-reduce | flops 1024 | bytes 8192 | tf_op jit(solution)/shard_map/psum | solution.py:28
  94.4 0.0 copy-done.2
  94.4 0.0 copy-start.3
  94.5 2.3 fusion.1
  96.7 0.0 copy-done.3
  96.7 0.0 copy-start.4
  96.7 2.0 convolution_convert_fusion.1
  98.8 0.0 copy-done.4
  98.8 2.0 convolution_convert_fusion.2
  100.8 2.1 pad_maximum_fusion
  102.9 0.0 all-reduce.2.cloned.1.call-update
  102.9 0.0 reduce-scatter.2.cloned.1.call-start
  103.0 121.4 %all-reduce.2.cloned.1.call-done = bf16[1024,1664]{0,1:T(8,128)(2,1)} async-done(((bf16[1024,1664]{0,1:T(8,128)(2,1)}), bf16[1024,1664]{0,1:T(8,128)(2,1)}) %all-reduce.2.cloned.1.call-update) | async-done | bytes 3407888 | tf_op jit(solution)/shard_map/psum | solution.py:30
  224.3 2.8 convert_element_type.26
  227.1 0.0 copy-done
  227.1 3.9 convolution_convert_fusion
  231.0 0.0 reduce-scatter.2.cloned.1.call-update
  231.0 224.9 %reduce-scatter.2.cloned.1.call-done = bf16[32,1024]{1,0:T(8,128)(2,1)} async-done(((bf16[1024,1024]{1,0:T(8,128)(2,1)}), bf16[32,1024]{1,0:T(8,128)(2,1)}) %reduce-scatter.2.cloned.1.call-update) | async-done | bytes 65552 | tf_op jit(solution)/shard_map/reduce_scatter | solution.py:34
  (1 shorter events, 0.0 us)
Async XLA Ops:
  6.5 220.6 %copy-start = (bf16[832,1024]{1,0:T(8,128)(2,1)S(1)}, bf16[832,1024]{1,0:T(8,128)(2,1)}, u32[]{:S(2)}) copy-start(bf16[832,1024]{1,0:T(8,128)(2,1)} %param.9) | copy-start | bytes 5111812
  6.5 217.8 %all-reduce.2.cloned.1.call-start = ((), (), s32[]{:S(2)}) async-start(), calls=%async_computation.2 | async-start | bytes 6815744 | tf_op jit(solution)/shard_map/psum | solution.py:30
  71.3 1.4 copy-start.1
  72.6 21.8 %copy-start.2 = (f32[1024]{0:T(1024)S(1)}, f32[1024]{0:T(1024)}, u32[]{:S(2)}) copy-start(f32[1024]{0:T(1024)} %param.6) | copy-start | bytes 12292
  94.4 2.3 copy-start.3
  96.7 2.0 copy-start.4
  102.9 353.0 %reduce-scatter.2.cloned.1.call-start = ((), (), s32[]{:S(2)}) async-start(), calls=%async_computation.3 | async-start | bytes 2162688 | tf_op jit(solution)/shard_map/reduce_scatter | solution.py:34
Sparse Core Ops, SparseCore 0:
  103.0 121.2 all-reduce.1
  231.1 224.7 reduce-scatter.1
